TPU v7x, 32 devices: a whole 2x2x4 slice. The times are simulated.
32 devices in a mesh: dp: 8 (over z, core), leaf: 4 (over y, x).
Axes of the slice: x: 2, y: 2, z: 4, core: 2. Of those that a mesh axis runs over, the one named last changes fastest.
Arguments:
- features: bfloat16 [51200, 384], P(('dp', 'leaf')), may hold values from -6 to 6
- head_weight: bfloat16 [384, 1536], replicated, may hold values from -0.3125 to 0.3125
- gain: float32 [1536], replicated, may hold values from 0.5 to 1.5
- shift: float32 [1536], replicated, may hold values from -3 to 3
- node_weights: bfloat16 [4096, 1536], P('leaf'), may hold values from -0.15625 to 0.15625
- subtree_map: int32 [64], replicated, may hold values from 0 to 63, each once
- node_ids: int32 [512, 64], P('dp'), may hold values from -1 to 4095, as said below
Outputs:
- head_grad: float32 [384, 1536], P(None, 'dp')
- gain_grad: float32 [1536], P('dp')
- shift_grad: float32 [1536], P('dp')
- node_grad: float32 [4096, 1536], P('leaf', 'dp')
Inputs may be any that keep to these rules, and one draw needn't show every extreme that they name: `node_ids`: each image has 1 to 16 positive ids, all in one subtree, in its first columns, then -1; and 1 to 48 hard-negative ids in another subtree from column 16 on, then -1. Ids of one image are distinct. The first image has full counts.
All inputs are finite; a program needn't handle non-finite values.
Results may differ from a plain program's by a relative error of at most 0.0036.
Values may be sent and summed in bfloat16 or wider, within the bound.
No kernel may reach another device: no remote copies, remote signals or barrier semaphores. Data moves between devices by JAX's collectives and lax.ppermute only.
A program may use at most 128 MiB of HBM per device.

v0:
```python
import jax
import jax.numpy as jnp
from jax import lax
from jax.sharding import PartitionSpec as P

P_SIZE = 100
SUB_SIZE = 64
KPOS = 16


def slot_table(slot_rows, owned_rows, values_rows, slots_dev):
    column = jnp.arange(slots_dev, dtype=jnp.int32)[None, None, :]
    match = (slot_rows[:, :, None] == column) & owned_rows[:, :, None]
    return jnp.sum(jnp.where(match, values_rows[:, :, None], 0.0), axis=1)


def shards(features, head_weight, gain, shift, node_weights, subtree_map, node_ids):
    images_here = features.shape[0] // P_SIZE
    width = head_weight.shape[1]
    linear_scores = jnp.dot(features, head_weight, preferred_element_type=jnp.float32)
    shifted = gain * linear_scores + shift
    sig = jax.nn.sigmoid(shifted)
    active = shifted * sig
    embedded = jnp.mean(active.reshape(images_here, P_SIZE, width), axis=1).astype(jnp.bfloat16)
    grouped = lax.all_gather(embedded, "leaf", axis=0, tiled=True)
    slots_dev = node_weights.shape[0]
    valid_pair = node_ids >= 0
    safe_ids = jnp.where(valid_pair, node_ids, 0)
    subtree = safe_ids // SUB_SIZE
    matches = (
        subtree[:, :, None] == jnp.arange(subtree_map.shape[0], dtype=jnp.int32)[None, None, :]
    )
    placed = jnp.sum(jnp.where(matches, subtree_map[None, None, :], 0), axis=2)
    slot_row = placed * SUB_SIZE + safe_ids % SUB_SIZE
    owned = valid_pair & (slot_row // slots_dev == lax.axis_index("leaf"))
    local_slot = jnp.where(owned, slot_row % slots_dev, 0)
    scores = lax.dot_general(
        grouped, node_weights, (((1,), (1,)), ((), ())), preferred_element_type=jnp.float32
    )
    target = (jnp.arange(node_ids.shape[1]) < KPOS).astype(jnp.float32)
    hit_count = slot_table(local_slot, owned, jnp.ones(local_slot.shape, jnp.float32), slots_dev)
    positive = slot_table(
        local_slot, owned, jnp.broadcast_to(target[None, :], local_slot.shape), slots_dev
    )
    table = jnp.where(hit_count > 0.5, jax.nn.sigmoid(scores) - positive, 0.0).astype(jnp.bfloat16)
    grad_part = jnp.dot(table, node_weights, preferred_element_type=jnp.float32)
    emb_grad = lax.psum_scatter(grad_part, "leaf", scatter_dimension=0, tiled=True)
    column_ids = jnp.arange(slots_dev, dtype=jnp.int32)[None, None, :]
    pick = (local_slot[:, :, None] == column_ids) & owned[:, :, None]
    coef = jnp.sum(jnp.where(pick, table.astype(jnp.float32)[:, None, :], 0.0), axis=2).astype(
        jnp.bfloat16
    )
    columns = lax.all_to_all(grouped, "dp", split_axis=1, concat_axis=0, tiled=True)
    all_coef = lax.all_gather(coef, "dp", axis=0, tiled=True)
    all_slot = lax.all_gather(local_slot, "dp", axis=0, tiled=True)
    every_pair = jnp.ones(all_slot.shape, jnp.bool_)
    all_table = slot_table(all_slot, every_pair, all_coef.astype(jnp.float32), slots_dev).astype(
        jnp.bfloat16
    )
    node_grad = lax.dot_general(
        all_table, columns, (((0,), (0,)), ((), ())), preferred_element_type=jnp.float32
    )
    slope = (sig * (1.0 + shifted * (1.0 - sig))).reshape(images_here, P_SIZE, width)
    pixel_gradient = ((emb_grad / P_SIZE)[:, None, :] * slope).reshape(images_here * P_SIZE, width)
    lin_grad = (pixel_gradient * gain).astype(jnp.bfloat16)
    head_term = lax.dot_general(
        features, lin_grad, (((0,), (0,)), ((), ())), preferred_element_type=jnp.float32
    )
    gain_term = jnp.sum(pixel_gradient * linear_scores, axis=0)
    shift_term = jnp.sum(pixel_gradient, axis=0)
    split_sums = (
        lax.psum_scatter(head_term, "dp", scatter_dimension=1, tiled=True),
        lax.psum_scatter(gain_term, "dp", scatter_dimension=0, tiled=True),
        lax.psum_scatter(shift_term, "dp", scatter_dimension=0, tiled=True),
    )
    head_grad, gain_grad, shift_grad = lax.psum(
        (split_sums[0], split_sums[1], split_sums[2]), "leaf"
    )
    return (head_grad, gain_grad, shift_grad, node_grad)


def solution(mesh):
    in_specs = (P(("dp", "leaf"), None), P(), P(), P(), P("leaf", None), P(), P("dp", None))
    out_specs = (P(None, "dp"), P("dp"), P("dp"), P("leaf", "dp"))
    return jax.shard_map(shards, mesh=mesh, in_specs=in_specs, out_specs=out_specs, check_vma=False)
```

profile of v0, /device:TPU:0, one launch (start us, length us, event | category | flops | bytes accessed | tf_op | source)
XLA Modules:
  0.0 237.6 jit_solution(990321862324019750)
XLA Ops:
  7.2 0.0 copy-start
  7.2 0.0 reduce-scatter.3.cloned.1.call-start
  7.2 0.9 add_select_fusion.3
  8.2 11.9 %fusion.1 = (f32[1600,1536]{1,0:T(8,128)}, f32[1600,1536]{1,0:T(8,128)}) fusion(f32[1536]{0:T(1024)} %param.10, f32[1536]{0:T(1024)} %param.9, bf16[1600,384]{1,0:T(8,128)(2,1)} %param.7, bf16[384,1536]{1,0:T(8,128)(2,1)} %param.8), kind=kOutput, calls=%fused_computation.11 | convolution fusion | flops 1902182400 | bytes 22081536 | tf_op jit(solution)/shard_map/dot_general | solution.py:20
  20.1 10.0 %reshape.27 = f32[16,100,1536]{2,1,0:T(8,128)} reshape(f32[1600,1536]{1,0:T(8,128)} %get-tuple-element.15) | data formatting | bytes 19660800 | tf_op jit(solution)/shard_map/reshape | solution.py:24
  30.1 0.0 copy-start.4
  30.1 0.0 copy-start.1
  30.1 5.3 %reduce_sum.74 = f32[16,1536]{1,0:T(8,128)S(1)} reduce(f32[16,100,1536]{2,1,0:T(8,128)} %reshape.27, f32[]{:T(128)} %constant.65.clone.1), dimensions={1}, to_apply=%region_2.3 | reduce | flops 2433024 | bytes 9928708 | tf_op jit(solution)/shard_map/reduce_sum | solution.py:24
  35.5 10.2 %all_gather.9 = bf16[64,1536]{1,0:T(8,128)(2,1)S(1)} all-gather(bf16[16,1536]{1,0:T(8,128)(2,1)S(1)} %multiply_convert_fusion.4), channel_id=1, replica_groups=mesh['dp'=8,'leaf'=4] {'leaf'}, dimensions={0}, use_global_device_ids=true | all-gather | bytes 245760 | tf_op jit(solution)/shard_map/all_gather | solution.py:25
  45.6 0.0 copy-done.4
  45.6 1.8 select_reduce_fusion.4
  47.5 0.0 copy-done.1
  47.5 0.1 fusion.15
  47.6 9.4 %select_reduce_fusion.3 = (f32[64,1024]{1,0:T(8,128)S(1)}, f32[64,1024]{1,0:T(8,128)S(1)}) fusion(s32[64,64]{1,0:T(8,128)S(1)} %get-tuple-element.13, pred[64,64]{1,0:T(8,128)(4,1)S(1)} %get-tuple-element.14, f32[64]{0:T(128)S(1)} %compare_convert_fusion), kind=kLoop, calls=%fused_computation.4 | loop fusion | flops 25034752 | bytes 545024 | tf_op jit(solution)/shard_map/reduce_sum | solution.py:14
  56.9 0.0 copy-done
  56.9 1.8 fusion.21
  58.7 1.4 fusion.22
  60.1 0.0 reduce-scatter.3.cloned.1.call-update
  60.2 0.2 reduce-scatter.5.cloned.1.call-start
  60.4 24.7 %reduce-scatter.3.cloned.1.call-done = f32[16,1536]{1,0:T(8,128)} async-done(((f32[64,1536]{1,0:T(8,128)}), f32[16,1536]{1,0:T(8,128)}) %reduce-scatter.3.cloned.1.call-update) | async-done | bytes 98320 | tf_op jit(solution)/shard_map/reduce_scatter | solution.py:47
  85.1 0.9 broadcast_multiply_fusion
  86.0 5.2 %mul.45 = f32[16,100,1536]{2,1,0:T(8,128)} broadcast(f32[16,1536]{1,0:T(8,128)S(1)} %broadcast_multiply_fusion), dimensions={0,2} | broadcast | bytes 9928704 | tf_op jit(solution)/shard_map/mul | solution.py:64
  91.1 0.0 copy-start.2
  91.2 0.0 copy-start.3
  91.2 10.0 %mul.46 = f32[1600,1536]{1,0:T(8,128)} reshape(f32[16,100,1536]{2,1,0:T(8,128)} %mul.45) | data formatting | bytes 19660800 | tf_op jit(solution)/shard_map/mul | solution.py:64
  101.2 0.0 copy-done.2
  101.2 0.0 copy-done.3
  101.2 0.0 copy-start.5
  101.2 9.0 %fusion.20 = (f32[1536]{0:T(1024)S(1)}, f32[1536]{0:T(1024)S(1)}, f32[1600,1536]{1,0:T(8,128)S(1)}) fusion(f32[1600,1536]{1,0:T(8,128)} %get-tuple-element.16, f32[1600,1536]{1,0:T(8,128)} %mul.46, f32[1536]{0:T(1024)S(1)} %copy-done.2, f32[1536]{0:T(1024)S(1)} %copy-done.3), kind=kLoop, calls=%fused_computation.52 | loop fusion | flops 31945728 | bytes 29515776 | tf_op jit(solution)/shard_map/reduce_sum | solution.py:70
  110.2 0.0 copy-done.5
  110.3 0.0 copy-start.6
  110.3 4.5 %fusion.4 = f32[384,1536]{0,1:T(8,128)} fusion(bf16[1600,384]{1,0:T(8,128)(2,1)S(1)} %copy-done.5, f32[1600,1536]{1,0:T(8,128)S(1)} %get-tuple-element.12, f32[1536]{0:T(1024)S(1)} %copy-done.3), kind=kOutput, calls=%fused_computation.15 | convolution fusion | flops 1892352000 | bytes 13424640 | tf_op jit(solution)/shard_map/dot_general | solution.py:66
  114.7 0.0 reduce-scatter.5.cloned.1.call-update
  114.8 0.9 all_to_all.14
  115.7 1.7 copy.13
  117.4 4.6 %all-to-all-start = ((bf16[64,8,192]{2,0,1:T(8,128)(2,1)}), bf16[64,8,192]{2,0,1:T(8,128)(2,1)}, u32[]{:S(2)}, u32[]{:S(2)}) async-start(bf16[64,8,192]{2,0,1:T(8,128)(2,1)} %copy.13), calls=%async_computation.2 | async-start | bytes 524288 | tf_op jit(solution)/shard_map/all_to_all | solution.py:53
  122.0 0.0 all-reduce.6.cloned.1.call-start
  122.1 5.3 %select_reduce_fusion.1 = bf16[64,64]{1,0:T(8,128)(2,1)S(1)} fusion(f32[64,1024]{1,0:T(8,128)} %get-tuple-element.17, s32[64,64]{1,0:T(8,128)S(1)} %get-tuple-element.13, pred[64,64]{1,0:T(8,128)(4,1)S(1)} %get-tuple-element.14), kind=kLoop, calls=%fused_computation.2 | loop fusion | flops 16773120 | bytes 290816 | tf_op jit(solution)/shard_map/reduce_sum | solution.py:50
  127.4 16.8 %all_gather.11 = bf16[512,64]{1,0:T(8,128)(2,1)S(1)} all-gather(bf16[64,64]{1,0:T(8,128)(2,1)S(1)} %select_reduce_fusion.1), channel_id=1, replica_groups=mesh['dp'=8,'leaf'=4] {'dp'}, dimensions={0}, use_global_device_ids=true | all-gather | bytes 73728 | tf_op jit(solution)/shard_map/all_gather | solution.py:54
  144.3 15.8 %all_gather.10 = s32[512,64]{1,0:T(8,128)} all-gather(s32[64,64]{1,0:T(8,128)S(1)} %get-tuple-element.13), channel_id=1, replica_groups=mesh['dp'=8,'leaf'=4] {'dp'}, dimensions={0}, use_global_device_ids=true | all-gather | bytes 147456 | tf_op jit(solution)/shard_map/all_gather | solution.py:55
  160.1 0.0 reduce-scatter.5.cloned.1.call-done
  160.1 0.0 all-reduce.6.cloned.1.call-update
  160.1 28.2 %select_reduce_fusion = bf16[512,1024]{1,0:T(8,128)(2,1)} fusion(f32[512,64]{1,0:T(8,128)S(1)} %convert_element_type.30, s32[512,64]{1,0:T(8,128)} %all_gather.10), kind=kLoop, calls=%fused_computation | loop fusion | flops 100139008 | bytes 1310720 | tf_op jit(solution)/shard_map/reduce_sum | solution.py:14
  188.3 0.0 copy-done.6
  188.3 0.6 dynamic-slice
  189.6 0.0 all-to-all-done
  189.6 2.6 %fusion.23 = f32[1024,192]{0,1:T(8,128)} fusion(bf16[512,1024]{1,0:T(8,128)(2,1)} %select_reduce_fusion, bf16[512,192]{1,0:T(8,128)(2,1)} %bitcast.2), kind=kOutput, calls=%fused_computation.55 | convolution fusion | flops 201326592 | bytes 2031616 | tf_op jit(solution)/shard_map/dot_general | solution.py:60
  192.1 27.6 %all-reduce.2 = (f32[1536]{0:T(1024)S(1)}, f32[1536]{0:T(1024)S(1)}) all-reduce(f32[1536]{0:T(1024)S(1)} %get-tuple-element.5, f32[1536]{0:T(1024)S(1)} %get-tuple-element.4), channel_id=4, replica_groups=mesh['dp'=8,'leaf'=4] {'dp'}, use_global_device_ids=true, to_apply=%region_8.9.clone | all-reduce | flops 3072 | bytes 24576
  219.8 0.1 dynamic-slice.1
  219.8 0.1 dynamic-slice.3
  219.9 9.4 %all-reduce.3 = (f32[192]{0:T(256)}, f32[192]{0:T(256)}) all-reduce(f32[192]{0:T(256)S(1)} %dynamic-slice.1, f32[192]{0:T(256)S(1)} %dynamic-slice.3), channel_id=1, replica_groups=mesh['dp'=8,'leaf'=4] {'leaf'}, use_global_device_ids=true, to_apply=%region_9.10 | all-reduce | flops 384 | bytes 3072 | tf_op jit(solution)/shard_map/psum | solution.py:76
  229.4 0.0 all-reduce.6.cloned.1.call-done
  229.4 1.7 copy.15
  (3 shorter events, 0.0 us)
Async XLA Ops:
  7.2 49.8 %copy-start = (bf16[1024,1536]{1,0:T(8,128)(2,1)S(1)}, bf16[1024,1536]{1,0:T(8,128)(2,1)}, u32[]{:S(2)}) copy-start(bf16[1024,1536]{1,0:T(8,128)(2,1)} %param.11) | copy-start | bytes 9437188
  7.2 77.9 %reduce-scatter.3.cloned.1.call-start = ((), (), s32[]{:S(2)}) async-start(), calls=%async_computation.3 | async-start | bytes 491520 | tf_op jit(solution)/shard_map/reduce_scatter | solution.py:47
  30.1 15.5 %copy-start.4 = (s32[64]{0:T(128)S(1)}, s32[64]{0:T(128)}, u32[]{:S(2)}) copy-start(s32[64]{0:T(128)} %param.12) | copy-start | bytes 772
  30.1 17.3 %copy-start.1 = (s32[64,64]{1,0:T(8,128)S(1)}, s32[64,64]{1,0:T(8,128)}, u32[]{:S(2)}) copy-start(s32[64,64]{1,0:T(8,128)} %param.13) | copy-start | bytes 49156
  60.2 99.9 %reduce-scatter.5.cloned.1.call-start = ((), (), s32[]{:S(2)}) async-start(), calls=%async_computation.4 | async-start | bytes 2654208 | tf_op jit(solution)/shard_map/reduce_scatter | solution.py:72
  91.1 10.1 %copy-start.2 = (f32[1536]{0:T(1024)S(1)}, f32[1536]{0:T(1024)}, u32[]{:S(2)}) copy-start(f32[1536]{0:T(1024)} %param.10) | copy-start | bytes 18436
  91.2 10.1 %copy-start.3 = (f32[1536]{0:T(1024)S(1)}, f32[1536]{0:T(1024)}, u32[]{:S(2)}) copy-start(f32[1536]{0:T(1024)} %param.9) | copy-start | bytes 18436
  101.2 9.0 %copy-start.5 = (bf16[1600,384]{1,0:T(8,128)(2,1)S(1)}, bf16[1600,384]{1,0:T(8,128)(2,1)}, u32[]{:S(2)}) copy-start(bf16[1600,384]{1,0:T(8,128)(2,1)} %param.7) | copy-start | bytes 3686404
  110.3 78.1 %copy-start.6 = (u32[32]{0:T(128)S(1)}, u32[32]{0:T(128)}, u32[]{:S(2)}) copy-start(u32[32]{0:T(128)} %constant.71) | copy-start | bytes 388
  117.4 72.2 %all-to-all-start = ((bf16[64,8,192]{2,0,1:T(8,128)(2,1)}), bf16[64,8,192]{2,0,1:T(8,128)(2,1)}, u32[]{:S(2)}, u32[]{:S(2)}) async-start(bf16[64,8,192]{2,0,1:T(8,128)(2,1)} %copy.13), calls=%async_computation.2 | async-start | bytes 524288 | tf_op jit(solution)/shard_map/all_to_all | solution.py:53
  122.0 107.4 %all-reduce.6.cloned.1.call-start = ((), (), s32[]{:S(2)}) async-start(), calls=%async_computation.5 | async-start | bytes 589824 | tf_op jit(solution)/shard_map/psum | solution.py:76
Sparse Core Ops, SparseCore 0:
  60.3 24.7 reduce-scatter.2
  114.9 41.0 reduce-scatter.4
  160.2 41.8 all-reduce.5
where the time goes:
time: 239 us; the launch traced here: 238 us
  blocking collectives  79.9 us (33%)
  other arithmetic  61 us (26%)
  local copies, waits for them, and re-layouts  30.4 us (13%)
  waiting for transfers between devices  24.7 us (10%)
  matrix products  22.2 us (9%)
  between operations  14.5 us (6%)
  starting transfers between devices  4.89 us (2%)
    reduce_sum x2, other arithmetic, slot_table(): return jnp.sum(jnp.where(match, values_rows[:, :, None], 0.0), axis=1)  37.6 us
    unnamed x1, blocking collectives  27.6 us
    reduce_scatter x1, waiting for transfers between devices, shards(): lax.psum_scatter(grad_part, 'leaf', scatter_dimension=0, tiled=True)  24.7 us
    all_gather x1, blocking collectives, shards(): all_coef = lax.all_gather(coef, 'dp', axis=0, tiled=True)  16.8 us
    all_gather x1, blocking collectives, shards(): all_slot = lax.all_gather(local_slot, 'dp', axis=0, tiled=True)  15.8 us
    mul x2, local copies, waits for them, and re-layouts, shards(): (emb_grad / P_SIZE)[:, None, :] * slope  15.2 us
    dot_general x1, matrix products, shards(): jnp.dot(features, head_weight, preferred_element_type=jnp.float32)  11.9 us
    all_gather x1, blocking collectives, shards(): grouped = lax.all_gather(embedded, 'leaf', axis=0, tiled=True)  10.2 us
  transfers between devices with their start and end apart: 4, of which 1 were waited for; matrix products, arithmetic and copies ran while one was open for 16% of the time, Pallas kernels for 0%

commit v1 on v0

--- a/solution.py
+++ b/solution.py
@@ -6,6 +6,17 @@
 P_SIZE = 100
 SUB_SIZE = 64
 KPOS = 16
+
+
+def collect(value, axis, dim):
+    ways = lax.axis_size(axis)
+    pieces = [value]
+    for far in range(1, ways):
+        pieces.append(
+            lax.ppermute(pieces[far - 1], axis, [(d, (d - 1) % ways) for d in range(ways)])
+        )
+    line = jnp.concatenate(pieces, axis=dim)
+    return jnp.roll(line, lax.axis_index(axis) * value.shape[dim], axis=dim)
 
 
 def slot_table(slot_rows, owned_rows, values_rows, slots_dev):
@@ -51,7 +62,7 @@
         jnp.bfloat16
     )
     columns = lax.all_to_all(grouped, "dp", split_axis=1, concat_axis=0, tiled=True)
-    all_coef = lax.all_gather(coef, "dp", axis=0, tiled=True)
+    all_coef = collect(coef, "dp", 0)
     all_slot = lax.all_gather(local_slot, "dp", axis=0, tiled=True)
     every_pair = jnp.ones(all_slot.shape, jnp.bool_)
     all_table = slot_table(all_slot, every_pair, all_coef.astype(jnp.float32), slots_dev).astype(

time: 239 us -> 267 us (1.12)
  starting transfers between devices: 4.89 us -> 25.5 us
  local copies, waits for them, and re-layouts: 30.4 us -> 40.1 us
  blocking collectives: 79.9 us -> 71.2 us
  waiting for transfers between devices: 24.7 us -> 29.8 us
    ppermute x0 -> x7, starting transfers between devices: none -> 21.1 us  [collect(): lax.ppermute(pieces[far - 1], axis, [(d, (d - 1) % ways) for d in range(w...]
    all_gather x1 -> x0, blocking collectives: 16.8 us -> none  [shards(): all_coef = lax.all_gather(coef, 'dp', axis=0, tiled=True)]
    unnamed x18 -> x33, local copies, waits for them, and re-layouts: 2.46 us -> 11.6 us
    all_gather x1, blocking collectives: 15.8 us -> 22.1 us  [shards(): all_slot = lax.all_gather(local_slot, 'dp', axis=0, tiled=True)]
    ppermute x0 -> x7, waiting for transfers between devices: none -> 5.02 us  [collect(): lax.ppermute(pieces[far - 1], axis, [(d, (d - 1) % ways) for d in range(w...]
  transfers between devices with their start and end apart: 4 -> 11, of which waited for: 1 -> 7; matrix products, arithmetic and copies ran while one was open for 16% -> 19% of each run, Pallas kernels for 0% -> 0%
where the time goes in v1:
time: 267 us; the launch traced here: 266 us
  blocking collectives  71.2 us (27%)
  other arithmetic  62.7 us (23%)
  local copies, waits for them, and re-layouts  40.1 us (15%)
  waiting for transfers between devices  29.8 us (11%)
  starting transfers between devices  25.5 us (10%)
  matrix products  22.2 us (8%)
  between operations  14.6 us (5%)
    reduce_sum x2, other arithmetic, slot_table(): return jnp.sum(jnp.where(match, values_rows[:, :, None], 0.0), axis=1)  37.6 us
    unnamed x1, blocking collectives  29.3 us
    reduce_scatter x1, waiting for transfers between devices, shards(): lax.psum_scatter(grad_part, 'leaf', scatter_dimension=0, tiled=True)  24.7 us
    all_gather x1, blocking collectives, shards(): all_slot = lax.all_gather(local_slot, 'dp', axis=0, tiled=True)  22.1 us
    ppermute x7, starting transfers between devices, collect(): lax.ppermute(pieces[far - 1], axis, [(d, (d - 1) % ways) for d in range(w...  21.1 us
    mul x2, local copies, waits for them, and re-layouts, shards(): (emb_grad / P_SIZE)[:, None, :] * slope  15.2 us
    dot_general x1, matrix products, shards(): jnp.dot(features, head_weight, preferred_element_type=jnp.float32)  11.9 us
    unnamed x33, local copies, waits for them, and re-layouts  11.6 us
  transfers between devices with their start and end apart: 11, of which 7 were waited for; matrix products, arithmetic and copies ran while one was open for 19% of the time, Pallas kernels for 0%

profile of v1, /device:TPU:0, one launch (start us, length us, event | category | flops | bytes accessed | tf_op | source)
XLA Modules:
  0.0 265.9 jit_solution(1800237899603414398)
XLA Ops:
  7.2 0.0 reduce-scatter.3.cloned.1.call-start
  7.2 0.9 add_select_fusion.3
  8.2 11.9 %fusion.1 = (f32[1600,1536]{1,0:T(8,128)}, f32[1600,1536]{1,0:T(8,128)}) fusion(f32[1536]{0:T(1024)} %param.10, f32[1536]{0:T(1024)} %param.9, bf16[1600,384]{1,0:T(8,128)(2,1)} %param.7, bf16[384,1536]{1,0:T(8,128)(2,1)} %param.8), kind=kOutput, calls=%fused_computation.11 | convolution fusion | flops 1902182400 | bytes 22081536 | tf_op jit(solution)/shard_map/dot_general | solution.py:31
  20.1 10.0 %reshape.27 = f32[16,100,1536]{2,1,0:T(8,128)} reshape(f32[1600,1536]{1,0:T(8,128)} %get-tuple-element.15) | data formatting | bytes 19660800 | tf_op jit(solution)/shard_map/reshape | solution.py:35
  30.1 5.3 %reduce_sum.74 = f32[16,1536]{1,0:T(8,128)S(1)} reduce(f32[16,100,1536]{2,1,0:T(8,128)} %reshape.27, f32[]{:T(128)} %constant.86.clone.1), dimensions={1}, to_apply=%region_2.3 | reduce | flops 2433024 | bytes 9928708 | tf_op jit(solution)/shard_map/reduce_sum | solution.py:35
  35.5 10.2 %all_gather.6 = bf16[64,1536]{1,0:T(8,128)(2,1)S(1)} all-gather(bf16[16,1536]{1,0:T(8,128)(2,1)S(1)} %multiply_convert_fusion.4), channel_id=1, replica_groups=mesh['dp'=8,'leaf'=4] {'leaf'}, dimensions={0}, use_global_device_ids=true | all-gather | bytes 245760 | tf_op jit(solution)/shard_map/all_gather | solution.py:36
  45.6 1.8 select_reduce_fusion.4
  47.5 0.1 fusion.15
  47.6 9.4 %select_reduce_fusion.3 = (f32[64,1024]{1,0:T(8,128)S(1)}, f32[64,1024]{1,0:T(8,128)S(1)}) fusion(s32[64,64]{1,0:T(8,128)S(1)} %get-tuple-element.13, pred[64,64]{1,0:T(8,128)(4,1)S(1)} %get-tuple-element.14, f32[64]{0:T(128)S(1)} %compare_convert_fusion), kind=kLoop, calls=%fused_computation.4 | loop fusion | flops 25034752 | bytes 545024 | tf_op jit(solution)/shard_map/reduce_sum | solution.py:25
  56.9 1.8 fusion.21
  58.7 1.4 fusion.22
  60.2 0.2 reduce-scatter.5.cloned.1.call-start
  60.4 24.7 %reduce-scatter.3.cloned.1.call-done = f32[16,1536]{1,0:T(8,128)} async-done(((f32[64,1536]{1,0:T(8,128)}), f32[16,1536]{1,0:T(8,128)}) %reduce-scatter.3.cloned.1.call-update) | async-done | bytes 98320 | tf_op jit(solution)/shard_map/reduce_scatter | solution.py:58
  85.1 0.9 broadcast_multiply_fusion
  86.0 5.2 %mul.48 = f32[16,100,1536]{2,1,0:T(8,128)} broadcast(f32[16,1536]{1,0:T(8,128)S(1)} %broadcast_multiply_fusion), dimensions={0,2} | broadcast | bytes 9928704 | tf_op jit(solution)/shard_map/mul | solution.py:75
  91.2 10.0 %mul.49 = f32[1600,1536]{1,0:T(8,128)} reshape(f32[16,100,1536]{2,1,0:T(8,128)} %mul.48) | data formatting | bytes 19660800 | tf_op jit(solution)/shard_map/mul | solution.py:75
  101.2 9.0 %fusion.20 = (f32[1536]{0:T(1024)S(1)}, f32[1536]{0:T(1024)S(1)}, f32[1600,1536]{1,0:T(8,128)S(1)}) fusion(f32[1600,1536]{1,0:T(8,128)} %get-tuple-element.16, f32[1600,1536]{1,0:T(8,128)} %mul.49, f32[1536]{0:T(1024)S(1)} %copy-done.2, f32[1536]{0:T(1024)S(1)} %copy-done.3), kind=kLoop, calls=%fused_computation.69 | loop fusion | flops 31945728 | bytes 29515776 | tf_op jit(solution)/shard_map/reduce_sum | solution.py:81
  110.3 4.5 %fusion.4 = f32[384,1536]{0,1:T(8,128)} fusion(bf16[1600,384]{1,0:T(8,128)(2,1)S(1)} %copy-done.5, f32[1600,1536]{1,0:T(8,128)S(1)} %get-tuple-element.12, f32[1536]{0:T(1024)S(1)} %copy-done.3), kind=kOutput, calls=%fused_computation.15 | convolution fusion | flops 1892352000 | bytes 13424640 | tf_op jit(solution)/shard_map/dot_general | solution.py:77
  114.7 0.0 reduce-scatter.5.cloned.1.call-update
  114.8 5.3 %select_reduce_fusion.1 = bf16[64,64]{1,0:T(8,128)(2,1)S(1)} fusion(f32[64,1024]{1,0:T(8,128)} %get-tuple-element.17, s32[64,64]{1,0:T(8,128)S(1)} %get-tuple-element.13, pred[64,64]{1,0:T(8,128)(4,1)S(1)} %get-tuple-element.14), kind=kLoop, calls=%fused_computation.2 | loop fusion | flops 16773120 | bytes 290816 | tf_op jit(solution)/shard_map/reduce_sum | solution.py:61
  120.1 2.5 collective-permute-start
  122.6 0.9 all_to_all.14
  123.5 1.7 copy.13
  125.2 4.0 %all-to-all-start = ((bf16[64,8,192]{2,0,1:T(8,128)(2,1)}), bf16[64,8,192]{2,0,1:T(8,128)(2,1)}, u32[]{:S(2)}, u32[]{:S(2)}) async-start(bf16[64,8,192]{2,0,1:T(8,128)(2,1)} %copy.13), calls=%async_computation.2 | async-start | bytes 524288 | tf_op jit(solution)/shard_map/all_to_all | solution.py:64
  129.3 0.0 all-reduce.6.cloned.1.call-start
  129.3 0.6 constant_dynamic-update-slice_fusion.15
  130.0 22.1 %all_gather.7 = s32[512,64]{1,0:T(8,128)S(1)} all-gather(s32[64,64]{1,0:T(8,128)S(1)} %get-tuple-element.13), channel_id=1, replica_groups=mesh['dp'=8,'leaf'=4] {'dp'}, dimensions={0}, use_global_device_ids=true | all-gather | bytes 147456 | tf_op jit(solution)/shard_map/all_gather | solution.py:66
  152.1 0.6 dynamic-slice
  153.3 1.1 collective-permute-start.1
  154.4 0.6 constant_dynamic-update-slice_fusion.14
  155.0 0.8 collective-permute-done.1
  155.8 3.5 %collective-permute-start.2 = (bf16[64,64]{1,0:T(8,128)(2,1)S(1)}, bf16[64,64]{1,0:T(8,128)(2,1)S(1)}, u32[]{:S(2)}, u32[]{:S(2)}) collective-permute-start(bf16[64,64]{1,0:T(8,128)(2,1)S(1)} %collective-permute-done.1), channel_id=1, source_target_pairs={{0,28},{4,0},{8,4},{12,8},{16,12},{20,16},{24,20},{28,24},{1,29},{... | collective-permute-start | bytes 24584 | tf_op jit(solution)/shard_map/ppermute | solution.py:16
  159.3 0.6 constant_dynamic-update-slice_fusion.13
  159.9 0.8 collective-permute-done.2
  160.8 3.5 %collective-permute-start.3 = (bf16[64,64]{1,0:T(8,128)(2,1)S(1)}, bf16[64,64]{1,0:T(8,128)(2,1)S(1)}, u32[]{:S(2)}, u32[]{:S(2)}) collective-permute-start(bf16[64,64]{1,0:T(8,128)(2,1)S(1)} %collective-permute-done.2), channel_id=1, source_target_pairs={{0,28},{4,0},{8,4},{12,8},{16,12},{20,16},{24,20},{28,24},{1,29},{... | collective-permute-start | bytes 24584 | tf_op jit(solution)/shard_map/ppermute | solution.py:16
  164.3 0.6 constant_dynamic-update-slice_fusion.12
  164.9 0.8 collective-permute-done.3
  165.7 3.5 %collective-permute-start.4 = (bf16[64,64]{1,0:T(8,128)(2,1)S(1)}, bf16[64,64]{1,0:T(8,128)(2,1)S(1)}, u32[]{:S(2)}, u32[]{:S(2)}) collective-permute-start(bf16[64,64]{1,0:T(8,128)(2,1)S(1)} %collective-permute-done.3), channel_id=1, source_target_pairs={{0,28},{4,0},{8,4},{12,8},{16,12},{20,16},{24,20},{28,24},{1,29},{... | collective-permute-start | bytes 24584 | tf_op jit(solution)/shard_map/ppermute | solution.py:16
  169.3 0.6 constant_dynamic-update-slice_fusion.11
  169.9 0.8 collective-permute-done.4
  170.7 3.5 %collective-permute-start.5 = (bf16[64,64]{1,0:T(8,128)(2,1)S(1)}, bf16[64,64]{1,0:T(8,128)(2,1)S(1)}, u32[]{:S(2)}, u32[]{:S(2)}) collective-permute-start(bf16[64,64]{1,0:T(8,128)(2,1)S(1)} %collective-permute-done.4), channel_id=1, source_target_pairs={{0,28},{4,0},{8,4},{12,8},{16,12},{20,16},{24,20},{28,24},{1,29},{... | collective-permute-start | bytes 24584 | tf_op jit(solution)/shard_map/ppermute | solution.py:16
  174.2 0.6 constant_dynamic-update-slice_fusion.10
  174.8 0.8 collective-permute-done.5
  175.7 3.5 %collective-permute-start.6 = (bf16[64,64]{1,0:T(8,128)(2,1)S(1)}, bf16[64,64]{1,0:T(8,128)(2,1)S(1)}, u32[]{:S(2)}, u32[]{:S(2)}) collective-permute-start(bf16[64,64]{1,0:T(8,128)(2,1)S(1)} %collective-permute-done.5), channel_id=1, source_target_pairs={{0,28},{4,0},{8,4},{12,8},{16,12},{20,16},{24,20},{28,24},{1,29},{... | collective-permute-start | bytes 24584 | tf_op jit(solution)/shard_map/ppermute | solution.py:16
  179.2 0.6 constant_dynamic-update-slice_fusion.9
  179.8 0.8 collective-permute-done.6
  180.6 0.6 constant_dynamic-update-slice_fusion.8
  181.2 0.6 constant_dynamic-update-slice_fusion.7
  181.8 0.6 constant_dynamic-update-slice_fusion.6
  182.4 0.6 constant_dynamic-update-slice_fusion.5
  183.1 0.6 constant_dynamic-update-slice_fusion.4
  183.7 0.6 constant_dynamic-update-slice_fusion.3
  184.3 0.6 constant_dynamic-update-slice_fusion.2
  184.9 0.6 constant_dynamic-update-slice_fusion.1
  185.5 0.6 constant_dynamic-update-slice_fusion
  186.1 1.6 dynamic-slice_convert_fusion
  187.7 0.0 all-reduce.6.cloned.1.call-update
  187.7 28.3 %select_reduce_fusion = bf16[512,1024]{1,0:T(8,128)(2,1)} fusion(f32[512,64]{1,0:T(8,128)} %dynamic-slice_convert_fusion, s32[512,64]{1,0:T(8,128)S(1)} %all_gather.7), kind=kLoop, calls=%fused_computation | loop fusion | flops 100139008 | bytes 1310720 | tf_op jit(solution)/shard_map/reduce_sum | solution.py:25
  216.0 2.6 fusion.23
  218.6 29.3 %all-reduce.2 = (f32[1536]{0:T(1024)S(1)}, f32[1536]{0:T(1024)S(1)}) all-reduce(f32[1536]{0:T(1024)S(1)} %get-tuple-element.5, f32[1536]{0:T(1024)S(1)} %get-tuple-element.4), channel_id=4, replica_groups=mesh['dp'=8,'leaf'=4] {'dp'}, use_global_device_ids=true, to_apply=%region_8.9.clone | all-reduce | flops 3072 | bytes 24576
  247.9 0.1 dynamic-slice.1
  247.9 0.1 dynamic-slice.3
  248.0 9.7 %all-reduce.3 = (f32[192]{0:T(256)}, f32[192]{0:T(256)}) all-reduce(f32[192]{0:T(256)S(1)} %dynamic-slice.1, f32[192]{0:T(256)S(1)} %dynamic-slice.3), channel_id=1, replica_groups=mesh['dp'=8,'leaf'=4] {'leaf'}, use_global_device_ids=true, to_apply=%region_9.10 | all-reduce | flops 384 | bytes 3072 | tf_op jit(solution)/shard_map/psum | solution.py:87
  257.7 1.7 copy.30
  (21 shorter events, 0.1 us)
Async XLA Ops:
  7.2 49.8 %copy-start = (bf16[1024,1536]{1,0:T(8,128)(2,1)S(1)}, bf16[1024,1536]{1,0:T(8,128)(2,1)}, u32[]{:S(2)}) copy-start(bf16[1024,1536]{1,0:T(8,128)(2,1)} %param.11) | copy-start | bytes 9437188
  7.2 77.9 %reduce-scatter.3.cloned.1.call-start = ((), (), s32[]{:S(2)}) async-start(), calls=%async_computation.3 | async-start | bytes 491520 | tf_op jit(solution)/shard_map/reduce_scatter | solution.py:58
  30.1 15.5 %copy-start.4 = (s32[64]{0:T(128)S(1)}, s32[64]{0:T(128)}, u32[]{:S(2)}) copy-start(s32[64]{0:T(128)} %param.12) | copy-start | bytes 772
  30.1 17.3 %copy-start.1 = (s32[64,64]{1,0:T(8,128)S(1)}, s32[64,64]{1,0:T(8,128)}, u32[]{:S(2)}) copy-start(s32[64,64]{1,0:T(8,128)} %param.13) | copy-start | bytes 49156
  60.2 127.5 %reduce-scatter.5.cloned.1.call-start = ((), (), s32[]{:S(2)}) async-start(), calls=%async_computation.4 | async-start | bytes 2654208 | tf_op jit(solution)/shard_map/reduce_scatter | solution.py:83
  91.1 10.1 %copy-start.2 = (f32[1536]{0:T(1024)S(1)}, f32[1536]{0:T(1024)}, u32[]{:S(2)}) copy-start(f32[1536]{0:T(1024)} %param.10) | copy-start | bytes 18436
  91.2 10.1 %copy-start.3 = (f32[1536]{0:T(1024)S(1)}, f32[1536]{0:T(1024)}, u32[]{:S(2)}) copy-start(f32[1536]{0:T(1024)} %param.9) | copy-start | bytes 18436
  101.2 9.0 %copy-start.5 = (bf16[1600,384]{1,0:T(8,128)(2,1)S(1)}, bf16[1600,384]{1,0:T(8,128)(2,1)}, u32[]{:S(2)}) copy-start(bf16[1600,384]{1,0:T(8,128)(2,1)} %param.7) | copy-start | bytes 3686404
  110.3 41.8 %copy-start.6 = (u32[32]{0:T(128)S(1)}, u32[32]{0:T(128)}, u32[]{:S(2)}) copy-start(u32[32]{0:T(128)} %constant.97) | copy-start | bytes 388
  120.1 33.2 %collective-permute-start = (bf16[64,64]{1,0:T(8,128)(2,1)S(1)}, bf16[64,64]{1,0:T(8,128)(2,1)S(1)}, u32[]{:S(2)}, u32[]{:S(2)}) collective-permute-start(bf16[64,64]{1,0:T(8,128)(2,1)S(1)} %select_reduce_fusion.1), channel_id=1, source_target_pairs={{0,28},{4,0},{8,4},{12,8},{16,12},{20,16},{24,20},{28,24},{1,29},{... | collective-permute-start | bytes 24584 | tf_op jit(solution)/shard_map/ppermute | solution.py:16
  125.2 90.8 %all-to-all-start = ((bf16[64,8,192]{2,0,1:T(8,128)(2,1)}), bf16[64,8,192]{2,0,1:T(8,128)(2,1)}, u32[]{:S(2)}, u32[]{:S(2)}) async-start(bf16[64,8,192]{2,0,1:T(8,128)(2,1)} %copy.13), calls=%async_computation.2 | async-start | bytes 524288 | tf_op jit(solution)/shard_map/all_to_all | solution.py:64
  129.3 128.4 %all-reduce.6.cloned.1.call-start = ((), (), s32[]{:S(2)}) async-start(), calls=%async_computation.5 | async-start | bytes 589824 | tf_op jit(solution)/shard_map/psum | solution.py:87
  153.3 2.5 collective-permute-start.1
  155.8 5.0 %collective-permute-start.2 = (bf16[64,64]{1,0:T(8,128)(2,1)S(1)}, bf16[64,64]{1,0:T(8,128)(2,1)S(1)}, u32[]{:S(2)}, u32[]{:S(2)}) collective-permute-start(bf16[64,64]{1,0:T(8,128)(2,1)S(1)} %collective-permute-done.1), channel_id=1, source_target_pairs={{0,28},{4,0},{8,4},{12,8},{16,12},{20,16},{24,20},{28,24},{1,29},{... | collective-permute-start | bytes 24584 | tf_op jit(solution)/shard_map/ppermute | solution.py:16
  160.8 5.0 %collective-permute-start.3 = (bf16[64,64]{1,0:T(8,128)(2,1)S(1)}, bf16[64,64]{1,0:T(8,128)(2,1)S(1)}, u32[]{:S(2)}, u32[]{:S(2)}) collective-permute-start(bf16[64,64]{1,0:T(8,128)(2,1)S(1)} %collective-permute-done.2), channel_id=1, source_target_pairs={{0,28},{4,0},{8,4},{12,8},{16,12},{20,16},{24,20},{28,24},{1,29},{... | collective-permute-start | bytes 24584 | tf_op jit(solution)/shard_map/ppermute | solution.py:16
  165.7 5.0 %collective-permute-start.4 = (bf16[64,64]{1,0:T(8,128)(2,1)S(1)}, bf16[64,64]{1,0:T(8,128)(2,1)S(1)}, u32[]{:S(2)}, u32[]{:S(2)}) collective-permute-start(bf16[64,64]{1,0:T(8,128)(2,1)S(1)} %collective-permute-done.3), channel_id=1, source_target_pairs={{0,28},{4,0},{8,4},{12,8},{16,12},{20,16},{24,20},{28,24},{1,29},{... | collective-permute-start | bytes 24584 | tf_op jit(solution)/shard_map/ppermute | solution.py:16
  170.7 5.0 %collective-permute-start.5 = (bf16[64,64]{1,0:T(8,128)(2,1)S(1)}, bf16[64,64]{1,0:T(8,128)(2,1)S(1)}, u32[]{:S(2)}, u32[]{:S(2)}) collective-permute-start(bf16[64,64]{1,0:T(8,128)(2,1)S(1)} %collective-permute-done.4), channel_id=1, source_target_pairs={{0,28},{4,0},{8,4},{12,8},{16,12},{20,16},{24,20},{28,24},{1,29},{... | collective-permute-start | bytes 24584 | tf_op jit(solution)/shard_map/ppermute | solution.py:16
  175.7 5.0 %collective-permute-start.6 = (bf16[64,64]{1,0:T(8,128)(2,1)S(1)}, bf16[64,64]{1,0:T(8,128)(2,1)S(1)}, u32[]{:S(2)}, u32[]{:S(2)}) collective-permute-start(bf16[64,64]{1,0:T(8,128)(2,1)S(1)} %collective-permute-done.5), channel_id=1, source_target_pairs={{0,28},{4,0},{8,4},{12,8},{16,12},{20,16},{24,20},{28,24},{1,29},{... | collective-permute-start | bytes 24584 | tf_op jit(solution)/shard_map/ppermute | solution.py:16
Sparse Core Ops, SparseCore 0:
  60.3 24.7 reduce-scatter.2
  114.9 41.1 reduce-scatter.4
  187.9 43.7 all-reduce.5
